TPU v7x, 256 devices: a whole 4x4x8 slice. The times are simulated.
256 devices in a mesh: seq: 32 (over z, y_lo, core), tp: 8 (over y_hi, x).
Axes of the slice: x: 4, y: 4 (y_hi: 2, y_lo: 2; y = y_hi * 2 + y_lo), z: 8, core: 2. Of those that a mesh axis runs over, the one named last changes fastest.
Arguments:
- qkv_se: bfloat16 [16384, 3, 4096], P('seq', None, 'tp'), may hold values from -6 to 6
- residual: bfloat16 [16384, 4096], P('seq', 'tp'), may hold values from -108 to 108
- taps_se: bfloat16 [256, 7], P('tp'), may hold values from -2 to 2
- skip_se: bfloat16 [4096], P('tp'), may hold values from 0.5 to 1.5
- w_out: bfloat16 [4096, 4096], P('tp', 'seq'), may hold values from -0.1875 to 0.1875
- norm_gain: bfloat16 [4096], replicated, may hold values from 0.5 to 1.5
- w_in: bfloat16 [4096, 3, 4096], P('seq', None, 'tp'), may hold values from -0.09375 to 0.09375
- taps_mr: bfloat16 [256, 128], P('tp'), may hold values from -0.5 to 0.5
- skip_mr: bfloat16 [4096], P('tp'), may hold values from 0.5 to 1.5
Outputs:
- mixed: bfloat16 [16384, 4096], P('seq', 'tp')
All inputs are finite; a program needn't handle non-finite values.
Results may differ from a plain program's by a relative error of at most 0.0085.
Values may be sent and summed in bfloat16 or wider, within the bound.
No kernel may reach another device: no remote copies, remote signals or barrier semaphores. Data moves between devices by JAX's collectives and lax.ppermute only.
A program may use at most 64 MiB of HBM per device.

v0:
```python
import jax
import jax.numpy as jnp
from jax import lax
from jax.sharding import PartitionSpec as P

GROUP = 16
SE_TAPS = 7
MR_TAPS = 128


norm_eps = 1e-05


def shifted(block, axis, distance):
    devices = range(lax.axis_size(axis))
    route = [(i - distance, i) for i in devices if i - distance in devices]
    return lax.ppermute(block, axis, route)


def toeplitz_pair(taps):
    offsets = lax.broadcasted_iota(jnp.int32, (MR_TAPS, MR_TAPS), 0) - lax.broadcasted_iota(
        jnp.int32, (MR_TAPS, MR_TAPS), 1
    )
    lag_ids = lax.broadcasted_iota(jnp.int32, (MR_TAPS, MR_TAPS, MR_TAPS), 0)
    picks = (jnp.remainder(offsets, MR_TAPS)[None] == lag_ids).astype(jnp.bfloat16)
    table = jnp.einsum("gj,jts->gts", taps, picks, preferred_element_type=jnp.float32).astype(
        jnp.bfloat16
    )
    lower = jnp.where(offsets[None] >= 0, table, jnp.zeros_like(table))
    upper = jnp.where(offsets[None] < 0, table, jnp.zeros_like(table))
    return (lower, upper)


def project_out(y_se, w_out):
    return jnp.dot(
        y_se, lax.all_gather(w_out, "seq", axis=1, tiled=True), preferred_element_type=jnp.float32
    )


def per_device(qkv_se, residual, taps_se, skip_se, w_out, norm_gain, w_in, taps_mr, skip_mr):
    row_count = qkv_se.shape[0]
    chan_width = qkv_se.shape[2]
    local_groups = chan_width // GROUP
    query_se = qkv_se[:, 0].astype(jnp.float32)
    u_se = (qkv_se[:, 1].astype(jnp.float32) * qkv_se[:, 2].astype(jnp.float32)).astype(
        jnp.bfloat16
    )
    incoming_se = shifted(u_se[row_count - (SE_TAPS - 1) :], "seq", 1)
    extended = jnp.concatenate([incoming_se, u_se], axis=0).astype(jnp.float32)
    per_channel = jnp.repeat(taps_se.astype(jnp.float32), GROUP, axis=0)
    conv_se = jnp.zeros((row_count, chan_width), jnp.float32)
    for tap_index in range(SE_TAPS):
        begin = SE_TAPS - 1 - tap_index
        conv_se = conv_se + per_channel[:, tap_index] * extended[begin : begin + row_count]
    y_se = (query_se * (conv_se + skip_se.astype(jnp.float32) * u_se.astype(jnp.float32))).astype(
        jnp.bfloat16
    )
    gain_full = norm_gain.astype(jnp.float32)
    partial_out = project_out(y_se, w_out)
    share = lax.psum_scatter(partial_out, "tp", scatter_dimension=1, tiled=True)
    stream = residual.astype(jnp.float32) + share
    squares = lax.psum(jnp.sum(stream * stream, axis=1), "tp")
    scale = lax.rsqrt(squares / (chan_width * lax.axis_size("tp")) + norm_eps)
    my_gain = lax.dynamic_slice_in_dim(gain_full, lax.axis_index("tp") * chan_width, chan_width, 0)
    normed = (stream * scale[:, None] * my_gain).astype(jnp.bfloat16)
    gathered = lax.all_gather(normed, "tp", axis=1, tiled=True)
    piece = lax.all_gather(w_in, "seq", axis=0, tiled=True)
    flat_piece = piece.reshape(piece.shape[0], 3 * chan_width)
    proj = jnp.dot(gathered, flat_piece, preferred_element_type=jnp.float32).reshape(
        row_count, 3, chan_width
    )
    query_mr = proj[:, 0]
    u_mr = (proj[:, 1] * proj[:, 2]).astype(jnp.bfloat16)
    lower, upper = toeplitz_pair(taps_mr)
    block_count = row_count // MR_TAPS
    blocks = u_mr.reshape(block_count, MR_TAPS, local_groups, GROUP)
    inside = jnp.einsum("gts,bsgc->btgc", lower, blocks, preferred_element_type=jnp.float32)
    tail_rows = shifted(blocks[block_count - 1], "seq", 1)
    earlier = jnp.concatenate([tail_rows[None], blocks[: block_count - 1]], axis=0)
    conv_mr = inside + jnp.einsum(
        "gts,bsgc->btgc", upper, earlier, preferred_element_type=jnp.float32
    )
    conv_mr = conv_mr.reshape(row_count, chan_width)
    return (query_mr * (conv_mr + skip_mr.astype(jnp.float32) * u_mr.astype(jnp.float32))).astype(
        jnp.bfloat16
    )


def solution(mesh):
    placed = (
        P("seq", None, "tp"),
        P("seq", "tp"),
        P("tp", None),
        P("tp"),
        P("tp", "seq"),
        P(),
        P("seq", None, "tp"),
        P("tp", None),
        P("tp"),
    )
    return jax.shard_map(
        per_device, mesh=mesh, in_specs=placed, out_specs=P("seq", "tp"), check_vma=False
    )
```

profile of v0, /device:TPU:105, one launch (start us, length us, event | category | flops | bytes accessed | tf_op | source)
XLA Modules:
  0.0 438.2 jit_solution(15193154201921998345)
XLA Ops:
  6.5 0.7 all-gather.4.cloned.1.call-update
  7.3 1.3 multiply_convert_fusion.1
  8.7 5.2 %collective-permute-start = (bf16[6,512]{1,0:T(8,128)(2,1)S(1)}, bf16[6,512]{1,0:T(8,128)(2,1)S(1)}, u32[]{:S(2)}, u32[]{:S(2)}) collective-permute-start(bf16[6,512]{1,0:T(8,128)(2,1)S(1)} %slice_bitcast_fusion.1), channel_id=1, source_target_pairs={{0,8},{8,16},{16,24},{24,32},{32,40},{40,48},{48,56},{56,64},{64,7... | collective-permute-start | bytes 18440 | tf_op jit(solution)/shard_map/ppermute | solution.py:17
  13.9 0.8 broadcast_in_dim.26
  14.6 0.1 reshape.75
  14.8 1.3 fusion.51
  16.1 0.2 maximum_convert_fusion
  16.3 65.7 %all-gather.4.cloned.1.call-done = bf16[512,4096]{1,0:T(8,128)(2,1)} async-done(((bf16[512,128]{1,0:T(8,128)(2,1)}), bf16[512,4096]{1,0:T(8,128)(2,1)}) %all-gather.4.cloned.1.call-update) | async-done | bytes 4194320 | tf_op jit(solution)/shard_map/all_gather | solution.py:36
  82.0 8.7 %fusion.22 = f32[512,4096]{1,0:T(8,128)} fusion(bf16[512,4096]{1,0:T(8,128)(2,1)} %all-gather.4.cloned.1.call-done, f32[518,512]{1,0:T(8,128)S(1)} %maximum_convert_fusion, f32[512]{0:T(512)S(1)} %convert_element_type.78, f32[512]{0:T(512)S(1)} %bitcast.74, f32[512]{0:T(512)S(1)} %bitcast.75, f32[512]{0:T(512)S(1)} %bitcast.76, f32[512]{0:T(512)S(1)} %bitcast.77, ...), kind=kOutput, calls=%fused_computation.42 | convolution fusion | flops 2152464384 | bytes 20987904 | tf_op jit(solution)/shard_map/dot_general | solution.py:35
  90.8 0.0 all-gather.8.cloned.1.call-start
  90.8 0.9 copy-done.2
  91.7 0.9 copy.24
  92.8 0.8 dynamic-slice_convert_fusion
  93.5 115.5 %reduce-scatter.2.cloned.1.call-done = f32[512,512]{1,0:T(8,128)} async-done(((f32[512,4096]{1,0:T(8,128)}), f32[512,512]{1,0:T(8,128)}) %reduce-scatter.2.cloned.1.call-update) | async-done | bytes 1048592 | tf_op jit(solution)/shard_map/reduce_scatter | solution.py:60
  209.1 1.4 multiply_reduce_fusion
  210.5 16.9 %psum.7 = f32[512]{0:T(512)S(1)} all-reduce(f32[512]{0:T(512)S(1)} %multiply_reduce_fusion), channel_id=1, replica_groups=mesh['seq'=32,'tp'=8] {'tp'}, use_global_device_ids=true, to_apply=%region_2.0 | all-reduce | flops 512 | bytes 4096 | tf_op jit(solution)/shard_map/psum | solution.py:62
  227.4 2.3 multiply_convert_fusion
  229.8 3.3 select_bitcast_fusion
  233.1 83.3 %all-gather.8.cloned.1.call-done = bf16[4096,3,512]{0,2,1:T(8,128)(2,1)} async-done(((bf16[128,3,512]{0,2,1:T(8,128)(2,1)}), bf16[4096,3,512]{0,2,1:T(8,128)(2,1)}) %all-gather.8.cloned.1.call-update) | async-done | bytes 12582928 | tf_op jit(solution)/shard_map/all_gather | solution.py:67
  316.4 81.6 %all-gather.6.cloned.1.call-done = bf16[512,4096]{1,0:T(8,128)(2,1)} async-done(((bf16[512,512]{1,0:T(8,128)(2,1)}), bf16[512,4096]{1,0:T(8,128)(2,1)}) %all-gather.6.cloned.1.call-update) | async-done | bytes 4194320 | tf_op jit(solution)/shard_map/all_gather | solution.py:66
  398.0 10.6 %fusion = f32[512,3,512]{0,2,1:T(8,128)S(1)} fusion(bf16[4096,3,512]{0,2,1:T(8,128)(2,1)} %all-gather.8.cloned.1.call-done, bf16[512,4096]{1,0:T(8,128)(2,1)} %all-gather.6.cloned.1.call-done), kind=kOutput, calls=%fused_computation | convolution fusion | flops 6442450944 | bytes 19922944 | tf_op jit(solution)/shard_map/dot_general | solution.py:69
  408.7 0.9 fusion.9
  409.6 2.1 convert_element_type.84
  411.7 1.6 slice.121
  413.2 7.2 %collective-permute-start.1 = (bf16[128,32,16]{0,2,1:T(8,128)(2,1)}, bf16[128,32,16]{0,2,1:T(8,128)(2,1)}, u32[]{:S(2)}, u32[]{:S(2)}) collective-permute-start(bf16[128,32,16]{0,2,1:T(8,128)(2,1)} %bitcast.18), channel_id=1, source_target_pairs={{0,8},{8,16},{16,24},{24,32},{32,40},{40,48},{48,56},{56,64},{64,7... | collective-permute-start | bytes 393224 | tf_op jit(solution)/shard_map/ppermute | solution.py:17
  420.4 3.2 fusion.20
  423.6 0.9 slice.102
  424.5 1.1 copy.27
  425.7 2.5 fusion.6
  428.1 0.4 copy.29
  428.6 1.0 fusion.8
  429.6 2.0 copy.30
  (26 shorter events, 0.3 us)
Async XLA Ops:
  6.5 223.3 %copy-start = (bf16[32,128]{1,0:T(8,128)(2,1)S(1)}, bf16[32,128]{1,0:T(8,128)(2,1)}, u32[]{:S(2)}) copy-start(bf16[32,128]{1,0:T(8,128)(2,1)} %param.16) | copy-start | bytes 24580
  6.5 9.6 %copy-start.3 = (bf16[512]{0:T(512)(128)(2,1)S(1)}, bf16[512]{0:T(512)(128)(2,1)}, u32[]{:S(2)}) copy-start(bf16[512]{0:T(512)(128)(2,1)} %param.12) | copy-start | bytes 3076
  6.5 75.5 %all-gather.4.cloned.1.call-start = ((), (), s32[]{:S(2)}) async-start(), calls=%async_computation.1 | async-start | bytes 4325376 | tf_op jit(solution)/shard_map/all_gather | solution.py:36
  7.3 201.8 %reduce-scatter.2.cloned.1.call-start = ((), (), s32[]{:S(2)}) async-start(), calls=%async_computation.2 | async-start | bytes 9437184 | tf_op jit(solution)/shard_map/reduce_scatter | solution.py:60
  8.7 7.5 %collective-permute-start = (bf16[6,512]{1,0:T(8,128)(2,1)S(1)}, bf16[6,512]{1,0:T(8,128)(2,1)S(1)}, u32[]{:S(2)}, u32[]{:S(2)}) collective-permute-start(bf16[6,512]{1,0:T(8,128)(2,1)S(1)} %slice_bitcast_fusion.1), channel_id=1, source_target_pairs={{0,8},{8,16},{16,24},{24,32},{32,40},{40,48},{48,56},{56,64},{64,7... | collective-permute-start | bytes 18440 | tf_op jit(solution)/shard_map/ppermute | solution.py:17
  90.7 1.0 copy-start.2
  90.7 118.3 %copy-start.1 = (bf16[512,512]{1,0:T(8,128)(2,1)S(1)}, bf16[512,512]{1,0:T(8,128)(2,1)}, u32[]{:S(2)}) copy-start(bf16[512,512]{1,0:T(8,128)(2,1)} %param.10) | copy-start | bytes 1572868
  90.8 138.9 %copy-start.4 = (bf16[512]{0:T(512)(128)(2,1)S(1)}, bf16[512]{0:T(512)(128)(2,1)}, u32[]{:S(2)}) copy-start(bf16[512]{0:T(512)(128)(2,1)} %param.17) | copy-start | bytes 3076
  90.8 225.7 %all-gather.8.cloned.1.call-start = ((), (), s32[]{:S(2)}) async-start(), calls=%async_computation.4 | async-start | bytes 12976128 | tf_op jit(solution)/shard_map/all_gather | solution.py:67
  92.7 305.3 %all-gather.6.cloned.1.call-start = ((), (), s32[]{:S(2)}) async-start(), calls=%async_computation.3 | async-start | bytes 4718592 | tf_op jit(solution)/shard_map/all_gather | solution.py:66
  409.6 14.0 %slice-start = ((bf16[512,1,512]{0,2,1:T(8,128)(2,1)}), bf16[384,1,512]{0,2,1:T(8,128)(2,1)S(1)}, s32[]{:S(2)}) async-start(bf16[512,1,512]{0,2,1:T(8,128)(2,1)} %fusion.9), calls=%async_computation.5 | async-start | bytes 786432 | tf_op jit(solution)/shard_map/slice | solution.py:79
  413.2 12.4 %collective-permute-start.1 = (bf16[128,32,16]{0,2,1:T(8,128)(2,1)}, bf16[128,32,16]{0,2,1:T(8,128)(2,1)}, u32[]{:S(2)}, u32[]{:S(2)}) collective-permute-start(bf16[128,32,16]{0,2,1:T(8,128)(2,1)} %bitcast.18), channel_id=1, source_target_pairs={{0,8},{8,16},{16,24},{24,32},{32,40},{40,48},{48,56},{56,64},{64,7... | collective-permute-start | bytes 393224 | tf_op jit(solution)/shard_map/ppermute | solution.py:17
Sparse Core Ops, SparseCore 0:
  9.1 72.8 all-gather.3
  90.9 118.1 reduce-scatter.1
  210.8 105.5 all-gather.7
  318.8 79.2 all-gather.5
where the time goes:
time: 439 us; the launch traced here: 438 us
  waiting for transfers between devices  347 us (79%)
  matrix products  28.3 us (6%)
  blocking collectives  16.9 us (4%)
  between operations  13.3 us (3%)
  starting transfers between devices  12.5 us (3%)
  local copies, waits for them, and re-layouts  10.9 us (2%)
  other arithmetic  9.38 us (2%)
    reduce_scatter x1, waiting for transfers between devices, per_device(): share = lax.psum_scatter(partial_out, 'tp', scatter_dimension=1, tiled=True)  116 us
    all_gather x1, waiting for transfers between devices, per_device(): piece = lax.all_gather(w_in, 'seq', axis=0, tiled=True)  83.3 us
    all_gather x1, waiting for transfers between devices, per_device(): gathered = lax.all_gather(normed, 'tp', axis=1, tiled=True)  81.6 us
    all_gather x1, waiting for transfers between devices, project_out(): lax.all_gather(w_out, 'seq', axis=1, tiled=True)  65.7 us
    psum x1, blocking collectives, per_device(): squares = lax.psum(jnp.sum(stream * stream, axis=1), 'tp')  16.9 us
    ppermute x2, starting transfers between devices, shifted(): return lax.ppermute(block, axis, route)  12.4 us
    dot_general x1, matrix products, per_device(): jnp.dot(gathered, flat_piece, preferred_element_type=jnp.float32)  10.6 us
  transfers between devices with their start and end apart: 6, of which 4 were waited for; matrix products, arithmetic and copies ran while one was open for 4% of the time, Pallas kernels for 0%

commit v1 on v0

--- a/solution.py
+++ b/solution.py
@@ -32,9 +32,11 @@
 
 
 def project_out(y_se, w_out):
-    return jnp.dot(
-        y_se, lax.all_gather(w_out, "seq", axis=1, tiled=True), preferred_element_type=jnp.float32
-    )
+    tp_size = lax.axis_size("tp")
+    stacked = lax.all_gather(w_out, "seq", axis=0, tiled=False)
+    per_tp = stacked.reshape(tp_size, stacked.shape[0] // tp_size, *stacked.shape[1:])
+    partial = jnp.einsum("tc,kjcf->ktjf", y_se, per_tp, preferred_element_type=jnp.float32)
+    return partial.reshape(tp_size, y_se.shape[0], -1)
 
 
 def per_device(qkv_se, residual, taps_se, skip_se, w_out, norm_gain, w_in, taps_mr, skip_mr):
@@ -57,18 +59,18 @@
     )
     gain_full = norm_gain.astype(jnp.float32)
     partial_out = project_out(y_se, w_out)
-    share = lax.psum_scatter(partial_out, "tp", scatter_dimension=1, tiled=True)
+    share = lax.psum_scatter(partial_out, "tp", scatter_dimension=0, tiled=True)[0]
     stream = residual.astype(jnp.float32) + share
     squares = lax.psum(jnp.sum(stream * stream, axis=1), "tp")
     scale = lax.rsqrt(squares / (chan_width * lax.axis_size("tp")) + norm_eps)
     my_gain = lax.dynamic_slice_in_dim(gain_full, lax.axis_index("tp") * chan_width, chan_width, 0)
     normed = (stream * scale[:, None] * my_gain).astype(jnp.bfloat16)
-    gathered = lax.all_gather(normed, "tp", axis=1, tiled=True)
+    gathered = lax.all_gather(normed, "tp", axis=0, tiled=False)
     piece = lax.all_gather(w_in, "seq", axis=0, tiled=True)
-    flat_piece = piece.reshape(piece.shape[0], 3 * chan_width)
-    proj = jnp.dot(gathered, flat_piece, preferred_element_type=jnp.float32).reshape(
-        row_count, 3, chan_width
-    )
+    flat_piece = piece.reshape(gathered.shape[0], chan_width, 3 * chan_width)
+    proj = jnp.einsum(
+        "ktf,kfn->tn", gathered, flat_piece, preferred_element_type=jnp.float32
+    ).reshape(row_count, 3, chan_width)
     query_mr = proj[:, 0]
     u_mr = (proj[:, 1] * proj[:, 2]).astype(jnp.bfloat16)
     lower, upper = toeplitz_pair(taps_mr)

time: 439 us -> 418 us (0.952)
  waiting for transfers between devices: 347 us -> 283 us
  local copies, waits for them, and re-layouts: 10.9 us -> 48.1 us
  matrix products: 28.3 us -> 33.2 us
    all_gather x2, waiting for transfers between devices: 147 us -> 107 us  [the longest x1 59 us: project_out(): stacked = lax.all_gather(w_out, 'seq', axis=0, tiled=False)]
    all_gather x1, waiting for transfers between devices: 83.3 us -> 57.4 us  [per_device(): piece = lax.all_gather(w_in, 'seq', axis=0, tiled=True)]
    all_gather x0 -> x1, local copies, waits for them, and re-layouts: none -> 17 us  [per_device(): piece = lax.all_gather(w_in, 'seq', axis=0, tiled=True)]
    unnamed x11 -> x9, local copies, waits for them, and re-layouts: 1.87 us -> 12.9 us
    reshape x0 -> x1, local copies, waits for them, and re-layouts: none -> 9.15 us  [project_out(): return partial.reshape(tp_size, y_se.shape[0], -1)]
    dot_general x2, matrix products: 19.3 us -> 24.2 us  [the longest x1 15.7 us: per_device(): jnp.einsum('ktf,kfn->tn', gathered, flat_piece, preferred_element_type=jn...]
  transfers between devices with their start and end apart: 6 -> 6, of which waited for: 4 -> 4; matrix products, arithmetic and copies ran while one was open for 4% -> 11% of each run, Pallas kernels for 0% -> 0%
where the time goes in v1:
time: 418 us; the launch traced here: 417 us
  waiting for transfers between devices  283 us (68%)
  local copies, waits for them, and re-layouts  48.1 us (12%)
  matrix products  33.2 us (8%)
  blocking collectives  17.1 us (4%)
  between operations  13.3 us (3%)
  starting transfers between devices  11.9 us (3%)
  other arithmetic  10 us (2%)
    reduce_scatter x1, waiting for transfers between devices, per_device(): lax.psum_scatter(partial_out, 'tp', scatter_dimension=0, tiled=True)[0]  118 us
    all_gather x1, waiting for transfers between devices, project_out(): stacked = lax.all_gather(w_out, 'seq', axis=0, tiled=False)  59 us
    all_gather x1, waiting for transfers between devices, per_device(): piece = lax.all_gather(w_in, 'seq', axis=0, tiled=True)  57.4 us
    all_gather x1, waiting for transfers between devices, per_device(): gathered = lax.all_gather(normed, 'tp', axis=0, tiled=False)  47.5 us
    psum x1, blocking collectives, per_device(): squares = lax.psum(jnp.sum(stream * stream, axis=1), 'tp')  17.1 us
    all_gather x1, local copies, waits for them, and re-layouts, per_device(): piece = lax.all_gather(w_in, 'seq', axis=0, tiled=True)  17 us
    dot_general x1, matrix products, per_device(): jnp.einsum('ktf,kfn->tn', gathered, flat_piece, preferred_element_type=jn...  15.7 us
    unnamed x9, local copies, waits for them, and re-layouts  12.9 us
  transfers between devices with their start and end apart: 6, of which 4 were waited for; matrix products, arithmetic and copies ran while one was open for 11% of the time, Pallas kernels for 0%

profile of v1, /device:TPU:105, one launch (start us, length us, event | category | flops | bytes accessed | tf_op | source)
XLA Modules:
  0.0 417.1 jit_solution(14830422946725181785)
XLA Ops:
  6.5 0.7 all-gather.8.cloned.1.call-update
  7.3 1.3 multiply_convert_fusion.1
  8.7 5.2 %collective-permute-start = (bf16[6,512]{1,0:T(8,128)(2,1)S(1)}, bf16[6,512]{1,0:T(8,128)(2,1)S(1)}, u32[]{:S(2)}, u32[]{:S(2)}) collective-permute-start(bf16[6,512]{1,0:T(8,128)(2,1)S(1)} %slice_bitcast_fusion.1), channel_id=1, source_target_pairs={{0,8},{8,16},{16,24},{24,32},{32,40},{40,48},{48,56},{56,64},{64,7... | collective-permute-start | bytes 18440 | tf_op jit(solution)/shard_map/ppermute | solution.py:17
  13.9 0.8 broadcast_in_dim.26
  14.8 1.3 fusion.54
  16.1 0.7 convert_element_type.78
  17.0 59.0 %all-gather.8.cloned.1.call-done = bf16[16384,128]{1,0:T(8,128)(2,1)} async-done(((bf16[512,128]{1,0:T(8,128)(2,1)}), bf16[16384,128]{1,0:T(8,128)(2,1)}) %all-gather.8.cloned.1.call-update) | async-done | bytes 4194320 | tf_op jit(solution)/shard_map/all_gather | solution.py:36
  76.0 8.5 %fusion.27 = f32[512,8,4,128]{0,3,2,1:T(8,128)} fusion(bf16[8,4,512,128]{3,2,1,0:T(8,128)(2,1)} %bitcast.104, f32[518,512]{1,0:T(8,128)S(1)} %maximum_convert_fusion, f32[512]{0:T(512)S(1)} %convert_element_type.78, f32[512]{0:T(512)S(1)} %bitcast.98, f32[512]{0:T(512)S(1)} %bitcast.99, f32[512]{0:T(512)S(1)} %bitcast.100, f32[512]{0:T(512)S(1)} %bitcast.101, ...), kind=kOutput, calls=%fused_computation.45 | convolution fusion | flops 2152464384 | bytes 20987904 | tf_op jit(solution)/shard_map/tc,kjcf->ktjf/dot_general | solution.py:38
  84.5 9.1 %copy.29 = f32[8,512,512]{2,1,0:T(8,128)} copy(f32[8,512,512]{1,2,0:T(8,128)} %bitcast.95) | data formatting | bytes 16777216 | tf_op jit(solution)/shard_map/reshape | solution.py:39
  93.7 0.7 all-gather.6.cloned.1.call-update
  94.5 0.8 dynamic-slice_convert_fusion
  95.2 118.1 %reduce-scatter.2.cloned.1.call-done = f32[1,512,512]{2,1,0:T(8,128)} async-done(((f32[8,512,512]{2,1,0:T(8,128)}), f32[1,512,512]{2,1,0:T(8,128)}) %reduce-scatter.2.cloned.1.call-update) | async-done | bytes 1048592 | tf_op jit(solution)/shard_map/reduce_scatter | solution.py:62
  213.3 1.4 multiply_reduce_fusion
  214.8 17.1 %psum.7 = f32[512]{0:T(512)S(1)} all-reduce(f32[512]{0:T(512)S(1)} %multiply_reduce_fusion), channel_id=1, replica_groups=mesh['seq'=32,'tp'=8] {'tp'}, use_global_device_ids=true, to_apply=%region_2.0 | all-reduce | flops 512 | bytes 4096 | tf_op jit(solution)/shard_map/psum | solution.py:64
  231.9 2.3 multiply_convert_fusion
  234.3 3.3 select_bitcast_fusion
  237.6 57.4 %all-gather.6.cloned.1.call-done = bf16[4096,3,512]{2,0,1:T(8,128)(2,1)} async-done(((bf16[128,3,512]{2,0,1:T(8,128)(2,1)}), bf16[4096,3,512]{2,0,1:T(8,128)(2,1)}) %all-gather.6.cloned.1.call-update) | async-done | bytes 12582928 | tf_op jit(solution)/shard_map/all_gather | solution.py:69
  294.9 17.0 %copy.30 = bf16[4096,3,512]{0,2,1:T(8,128)(2,1)} copy(bf16[4096,3,512]{2,0,1:T(8,128)(2,1)} %all-gather.6.cloned.1.call-done) | data formatting | bytes 25165824 | tf_op jit(solution)/shard_map/all_gather | solution.py:69
  312.0 12.9 %copy.47 = bf16[192,8,8,512]{3,2,1,0:T(8,128)(2,1)} copy(bf16[192,8,8,512]{3,1,2,0:T(8,128)(2,1)} %bitcast.93) | data formatting | bytes 25165824
  324.9 47.5 %all-gather.10.cloned.1.call-done = bf16[4096,512]{1,0:T(8,128)(2,1)} async-done(((bf16[512,512]{1,0:T(8,128)(2,1)}), bf16[4096,512]{1,0:T(8,128)(2,1)}) %all-gather.10.cloned.1.call-update) | async-done | bytes 4194320 | tf_op jit(solution)/shard_map/all_gather | solution.py:68
  372.4 15.7 %fusion.4 = f32[512,3,512]{0,2,1:T(8,128)S(1)} fusion(bf16[8,512,512,1]{2,1,0,3:T(8,128)(2,1)} %bitcast.105, bf16[3,512,512,8]{2,3,1,0:T(8,128)(2,1)} %bitcast.94), kind=kOutput, calls=%fused_computation.5 | convolution fusion | flops 6442450944 | bytes 19922944 | tf_op jit(solution)/shard_map/ktf,kfn->tn/dot_general | solution.py:71
  388.1 0.9 fusion.11
  389.1 2.1 convert_element_type.84
  391.2 1.6 slice.121
  392.7 6.5 %collective-permute-start.1 = (bf16[128,32,16]{0,2,1:T(8,128)(2,1)}, bf16[128,32,16]{0,2,1:T(8,128)(2,1)}, u32[]{:S(2)}, u32[]{:S(2)}) collective-permute-start(bf16[128,32,16]{0,2,1:T(8,128)(2,1)} %bitcast.26), channel_id=1, source_target_pairs={{0,8},{8,16},{16,24},{24,32},{32,40},{40,48},{48,56},{56,64},{64,7... | collective-permute-start | bytes 393224 | tf_op jit(solution)/shard_map/ppermute | solution.py:17
  399.3 3.2 fusion.22
  402.5 0.9 slice.102
  403.4 1.1 copy.34
  404.5 2.5 fusion.8
  407.0 0.4 copy.36
  407.5 1.0 fusion.10
  408.5 2.0 copy.37
  (26 shorter events, 0.5 us)
Async XLA Ops:
  6.5 227.7 %copy-start = (bf16[32,128]{1,0:T(8,128)(2,1)S(1)}, bf16[32,128]{1,0:T(8,128)(2,1)}, u32[]{:S(2)}) copy-start(bf16[32,128]{1,0:T(8,128)(2,1)} %param.16) | copy-start | bytes 24580
  6.5 69.5 %all-gather.8.cloned.1.call-start = ((), (), s32[]{:S(2)}) async-start(), calls=%async_computation.3 | async-start | bytes 4325376 | tf_op jit(solution)/shard_map/all_gather | solution.py:36
  7.3 206.1 %reduce-scatter.2.cloned.1.call-start = ((), (), s32[]{:S(2)}) async-start(), calls=%async_computation.1 | async-start | bytes 9437184 | tf_op jit(solution)/shard_map/reduce_scatter | solution.py:62
  8.7 8.1 %collective-permute-start = (bf16[6,512]{1,0:T(8,128)(2,1)S(1)}, bf16[6,512]{1,0:T(8,128)(2,1)S(1)}, u32[]{:S(2)}, u32[]{:S(2)}) collective-permute-start(bf16[6,512]{1,0:T(8,128)(2,1)S(1)} %slice_bitcast_fusion.1), channel_id=1, source_target_pairs={{0,8},{8,16},{16,24},{24,32},{32,40},{40,48},{48,56},{56,64},{64,7... | collective-permute-start | bytes 18440 | tf_op jit(solution)/shard_map/ppermute | solution.py:17
  93.7 119.7 %copy-start.2 = (bf16[512,512]{1,0:T(8,128)(2,1)S(1)}, bf16[512,512]{1,0:T(8,128)(2,1)}, u32[]{:S(2)}) copy-start(bf16[512,512]{1,0:T(8,128)(2,1)} %param.10) | copy-start | bytes 1572868
  93.7 140.5 %copy-start.3 = (bf16[512]{0:T(512)(128)(2,1)S(1)}, bf16[512]{0:T(512)(128)(2,1)}, u32[]{:S(2)}) copy-start(bf16[512]{0:T(512)(128)(2,1)} %param.17) | copy-start | bytes 3076
  93.7 201.2 %all-gather.6.cloned.1.call-start = ((), (), s32[]{:S(2)}) async-start(), calls=%async_computation.2 | async-start | bytes 12976128 | tf_op jit(solution)/shard_map/all_gather | solution.py:69
  94.4 278.0 %all-gather.10.cloned.1.call-start = ((), (), s32[]{:S(2)}) async-start(), calls=%async_computation.4 | async-start | bytes 4718592 | tf_op jit(solution)/shard_map/all_gather | solution.py:68
  389.1 13.4 %slice-start = ((bf16[512,1,512]{0,2,1:T(8,128)(2,1)}), bf16[384,1,512]{0,2,1:T(8,128)(2,1)S(1)}, s32[]{:S(2)}) async-start(bf16[512,1,512]{0,2,1:T(8,128)(2,1)} %fusion.11), calls=%async_computation.5 | async-start | bytes 786432 | tf_op jit(solution)/shard_map/slice | solution.py:81
  392.7 11.8 %collective-permute-start.1 = (bf16[128,32,16]{0,2,1:T(8,128)(2,1)}, bf16[128,32,16]{0,2,1:T(8,128)(2,1)}, u32[]{:S(2)}, u32[]{:S(2)}) collective-permute-start(bf16[128,32,16]{0,2,1:T(8,128)(2,1)} %bitcast.26), channel_id=1, source_target_pairs={{0,8},{8,16},{16,24},{24,32},{32,40},{40,48},{48,56},{56,64},{64,7... | collective-permute-start | bytes 393224 | tf_op jit(solution)/shard_map/ppermute | solution.py:17
  404.5 6.0 %copy-start.1 = (bf16[32,128]{1,0:T(8,128)(2,1)S(1)}, bf16[32,128]{1,0:T(8,128)(2,1)}, u32[]{:S(2)}) copy-start(bf16[32,128]{1,0:T(8,128)(2,1)} %param.16) | copy-start | bytes 24580
Sparse Core Ops, SparseCore 0:
  9.2 66.7 all-gather.7
  93.8 119.4 reduce-scatter.1
  215.2 79.6 all-gather.5
  297.4 74.9 all-gather.9
